TPU v7x, 256 devices: a whole 4x4x8 slice. The times are simulated.
256 devices in a mesh: shard: 8 (over z), tensor: 4 (over y), section: 8 (over x, core).
Axes of the slice: x: 4, y: 4, z: 8, core: 2. Of those that a mesh axis runs over, the one named last changes fastest.
Arguments:
- emb_grad: float32 [960, 32000], P(('tensor', 'section'), 'shard'), may hold values from -60 to 60
- mlp_grad: float32 [3, 960, 2560], P(None, ('tensor', 'section'), 'shard'), may hold values from -60 to 60
- emb_basis: float32 [960, 256], P(('tensor', 'section')), may hold values from -0.1875 to 0.1875
- mlp_basis: float32 [3, 960, 256], P(None, ('tensor', 'section')), may hold values from -0.1875 to 0.1875
- emb_first: float32 [256, 32000], P(('tensor', 'section'), 'shard'), may hold values from -6 to 6
- emb_second: float32 [256, 32000], P(('tensor', 'section'), 'shard'), may hold values from 0.002 to 0.05
- mlp_first: float32 [256, 3, 2560], P(('tensor', 'section'), None, 'shard'), may hold values from -6 to 6
- mlp_second: float32 [256, 3, 2560], P(('tensor', 'section'), None, 'shard'), may hold values from 0.002 to 0.05
Outputs:
- emb_update: float32 [960, 32000], P(('tensor', 'section'), 'shard')
- mlp_update: float32 [3, 960, 2560], P(None, ('tensor', 'section'), 'shard')
- emb_first_new: float32 [256, 32000], P(('tensor', 'section'), 'shard')
- emb_second_new: float32 [256, 32000], P(('tensor', 'section'), 'shard')
- mlp_first_new: float32 [256, 3, 2560], P(('tensor', 'section'), None, 'shard')
- mlp_second_new: float32 [256, 3, 2560], P(('tensor', 'section'), None, 'shard')
- emb_basis_new: float32 [960, 256], P(('tensor', 'section'))
- mlp_basis_new: float32 [3, 960, 256], P(None, ('tensor', 'section'))
All inputs are finite; a program needn't handle non-finite values.
Results may differ from a plain program's by a relative error of at most 0.0003.
Values sent between devices are 32-bit elements; how exact they have to be, the bound alone decides.
No kernel may reach another device: no remote copies, remote signals or barrier semaphores. Data moves between devices by JAX's collectives and lax.ppermute only.
A program may use at most 64 MiB of HBM per device.

v0:
```python
import jax
import jax.numpy as jnp
from jax import lax
from jax.sharding import PartitionSpec as P

NS_STEPS = 3
coef_a = 3.4445
coef_b = -4.775
coef_c = 2.0315
bias_one = 1.0 - 0.9**10
bias_two = 1.0 - 0.999**10
adam_eps = 1e-08
norm_eps = 1e-07
highest = lax.Precision.HIGHEST


def adam_moments(first, second, projected):
    first_new = 0.9 * first + 0.1 * projected
    second_new = 0.999 * second + 0.001 * projected * projected
    direction = first_new / bias_one / (jnp.sqrt(second_new / bias_two) + adam_eps)
    return (first_new, second_new, direction)


def newton_schulz(target, gram):
    squares = jnp.trace(gram, axis1=-2, axis2=-1)
    scale = 1.0 / (jnp.sqrt(squares) + norm_eps)
    gram_term = gram * (scale * scale)[..., None, None]
    eye = jnp.eye(gram.shape[-1], dtype=gram.dtype)
    total = None
    for sweep_index in range(NS_STEPS):
        factor = coef_a * eye + polish_poly(gram_term)
        if sweep_index + 1 < NS_STEPS:
            gram_term = jnp.einsum(
                "...rs,...st->...rt",
                factor,
                jnp.einsum("...rs,...st->...rt", gram_term, factor, precision=highest),
                precision=highest,
            )
        total = (
            factor
            if total is None
            else jnp.einsum("...rs,...st->...rt", total, factor, precision=highest)
        )
    current = target * scale[..., None, None]
    return jnp.einsum("...dr,...rs->...ds", current, total, precision=highest)


def polish_poly(gram_term):
    return coef_b * gram_term + coef_c * jnp.einsum(
        "...rs,...st->...rt", gram_term, gram_term, precision=highest
    )


def gram_sums(emb_iterate, mlp_iterate):
    emb_gram = jnp.einsum("dr,ds->rs", emb_iterate, emb_iterate, precision=highest)
    mlp_gram = jnp.einsum("kdr,kds->krs", mlp_iterate, mlp_iterate, precision=highest)
    return lax.psum((emb_gram, mlp_gram), ("tensor", "section"))


def local_terms(emb_grad, mlp_grad, emb_basis, mlp_basis):
    emb_term = jnp.einsum("dr,dv->rv", emb_basis, emb_grad, precision=highest)
    mlp_term = jnp.einsum("kdr,kdf->rkf", mlp_basis, mlp_grad, precision=highest)
    return (emb_term, mlp_term)


def project_back(emb_basis, mlp_basis, emb_total, mlp_total, emb_piece, mlp_piece):
    emb_total = jnp.dot(emb_basis, emb_piece, precision=highest)
    mlp_total = jnp.einsum("kdr,rkf->kdf", mlp_basis, mlp_piece, precision=highest)
    return (emb_total, mlp_total)


def local(emb_grad, mlp_grad, emb_basis, mlp_basis, emb_first, emb_second, mlp_first, mlp_second):
    emb_term, mlp_term = local_terms(emb_grad, mlp_grad, emb_basis, mlp_basis)
    emb_zero = jnp.zeros(emb_grad.shape, jnp.float32)
    mlp_zero = jnp.zeros(mlp_grad.shape, jnp.float32)
    emb_share, mlp_share = (
        lax.psum_scatter(emb_term, ("tensor", "section"), scatter_dimension=0, tiled=True),
        lax.psum_scatter(mlp_term, ("tensor", "section"), scatter_dimension=0, tiled=True),
    )
    emb_first_new, emb_second_new, emb_direction = adam_moments(emb_first, emb_second, emb_share)
    mlp_first_new, mlp_second_new, mlp_direction = adam_moments(mlp_first, mlp_second, mlp_share)
    emb_total = emb_zero
    mlp_total = mlp_zero
    emb_piece = lax.all_gather(emb_direction, ("tensor", "section"), axis=0, tiled=True)
    emb_projected = lax.all_gather(emb_share, ("tensor", "section"), axis=0, tiled=True)
    mlp_piece = lax.all_gather(mlp_direction, ("tensor", "section"), axis=0, tiled=True)
    mlp_projected = lax.all_gather(mlp_share, ("tensor", "section"), axis=0, tiled=True)
    emb_total, mlp_total = project_back(
        emb_basis, mlp_basis, emb_total, mlp_total, emb_piece, mlp_piece
    )
    emb_found_block = jnp.einsum("dv,rv->dr", emb_grad, emb_projected, precision=highest)
    mlp_found_block = jnp.einsum("kdf,rkf->kdr", mlp_grad, mlp_projected, precision=highest)
    emb_part, mlp_part = lax.psum((emb_found_block, mlp_found_block), "shard")
    emb_gram, mlp_gram = gram_sums(emb_part, mlp_part)
    emb_iterate = newton_schulz(emb_part, emb_gram)
    mlp_iterate = newton_schulz(mlp_part, mlp_gram)
    return (
        emb_total,
        mlp_total,
        emb_first_new,
        emb_second_new,
        mlp_first_new,
        mlp_second_new,
        emb_iterate,
        mlp_iterate,
    )


def solution(mesh):
    placed = (
        P(("tensor", "section"), "shard"),
        P(None, ("tensor", "section"), "shard"),
        P(("tensor", "section"), None),
        P(None, ("tensor", "section"), None),
        P(("tensor", "section"), "shard"),
        P(("tensor", "section"), "shard"),
        P(("tensor", "section"), None, "shard"),
        P(("tensor", "section"), None, "shard"),
    )
    return jax.shard_map(
        local,
        mesh=mesh,
        in_specs=placed,
        out_specs=(
            P(("tensor", "section"), "shard"),
            P(None, ("tensor", "section"), "shard"),
            P(("tensor", "section"), "shard"),
            P(("tensor", "section"), "shard"),
            P(("tensor", "section"), None, "shard"),
            P(("tensor", "section"), None, "shard"),
            P(("tensor", "section"), None),
            P(None, ("tensor", "section"), None),
        ),
        check_vma=False,
    )
```

profile of v0, /device:TPU:1, one launch (start us, length us, event | category | flops | bytes accessed | tf_op | source)
XLA Modules:
  0.0 548.8 jit_solution(6398069834945036047)
XLA Ops:
  7.2 2.0 convolution_bitcast_fusion.1
  9.3 1.5 copy.31
  10.9 5.1 fusion.34
  17.9 113.6 %all-reduce.8.cloned.1.call-done = f32[256,3,320]{2,1,0:T(4,128)} async-done(((f32[256,3,320]{2,1,0:T(4,128)}), f32[256,3,320]{2,1,0:T(4,128)}) %all-reduce.8.cloned.1.call-update) | async-done | bytes 983056
  133.0 26.2 %all_gather.15 = f32[256,3,320]{2,0,1:T(8,128)S(1)} all-gather(f32[8,3,320]{2,0,1:T(8,128)S(1)} %get-tuple-element.31), channel_id=1, replica_groups=mesh['shard'=8,'tensor'=4,'section'=8] {'tensor','section'}, dimensions={0}, use_global_device_ids=true | all-gather | bytes 1013760 | tf_op jit(solution)/shard_map/all_gather | solution.py:87
  159.2 1.8 convolution_bitcast_fusion.3
  161.2 62.4 %reduce-scatter.2.cloned.1.call-done = f32[8,4000]{1,0:T(8,128)} async-done(((f32[256,4000]{1,0:T(8,128)}), f32[8,4000]{1,0:T(8,128)}) %reduce-scatter.2.cloned.1.call-update) | async-done | bytes 128016 | tf_op jit(solution)/shard_map/reduce_scatter | solution.py:77
  223.7 1.7 add_divide_fusion
  225.5 26.8 %all_gather.13 = f32[256,3,320]{2,0,1:T(8,128)S(1)} all-gather(f32[8,3,320]{2,0,1:T(8,128)S(1)} %get-tuple-element.28), channel_id=1, replica_groups=mesh['shard'=8,'tensor'=4,'section'=8] {'tensor','section'}, dimensions={0}, use_global_device_ids=true | all-gather | bytes 1013760 | tf_op jit(solution)/shard_map/all_gather | solution.py:86
  252.3 42.7 %all-reduce.6.cloned.1.call-done = f32[3,30,256]{2,1,0:T(8,128)} async-done(((f32[3,30,256]{2,1,0:T(8,128)}), f32[3,30,256]{2,1,0:T(8,128)}) %all-reduce.6.cloned.1.call-update) | async-done | bytes 92176 | tf_op jit(solution)/shard_map/psum | solution.py:93
  295.0 2.8 fusion.41
  297.8 54.2 %all-gather.5.cloned.1.call-done = f32[256,4000]{1,0:T(8,128)} async-done(((f32[8,4000]{1,0:T(8,128)}), f32[256,4000]{1,0:T(8,128)}) %all-gather.5.cloned.1.call-update) | async-done | bytes 4096016 | tf_op jit(solution)/shard_map/all_gather | solution.py:85
  352.0 5.9 %convolution_bitcast_fusion.4 = f32[30,256]{1,0:T(8,128)S(1)} fusion(f32[256,4000]{1,0:T(8,128)} %all-gather.5.cloned.1.call-done, f32[30,4000]{1,0:T(8,128)S(1)} %copy-done), kind=kOutput, calls=%fused_computation.22 | convolution fusion | flops 368640000 | bytes 4606720 | tf_op jit(solution)/shard_map/dv,rv->dr/dot_general | solution.py:91
  357.9 23.7 %psum.28 = f32[30,256]{1,0:T(8,128)S(1)} all-reduce(f32[30,256]{1,0:T(8,128)S(1)} %convolution_bitcast_fusion.4), channel_id=1, replica_groups=mesh['shard'=8,'tensor'=4,'section'=8] {'shard'}, use_global_device_ids=true, to_apply=%region_2.0 | all-reduce | flops 7680 | bytes 61440 | tf_op jit(solution)/shard_map/psum | solution.py:93
  381.5 1.1 fusion.35
  382.7 1.4 convolution_bitcast_fusion.2
  384.1 21.4 %all-gather.3.cloned.1.call-done = f32[256,4000]{1,0:T(8,128)} async-done(((f32[8,4000]{1,0:T(8,128)}), f32[256,4000]{1,0:T(8,128)}) %all-gather.3.cloned.1.call-update) | async-done | bytes 4096016 | tf_op jit(solution)/shard_map/all_gather | solution.py:84
  405.5 5.5 %convolution_bitcast_fusion = f32[30,4000]{1,0:T(8,128)} fusion(f32[256,4000]{1,0:T(8,128)} %all-gather.3.cloned.1.call-done, f32[30,256]{1,0:T(8,128)S(1)} %copy-done.6), kind=kOutput, calls=%fused_computation | convolution fusion | flops 368640000 | bytes 4606720 | tf_op jit(solution)/shard_map/dot_general | solution.py:67
  411.0 112.1 %all-reduce.10.cloned.1.call-done = (f32[256,256]{1,0:T(8,128)}, f32[3,256,256]{2,1,0:T(8,128)}) async-done(((f32[256,256]{1,0:T(8,128)}, f32[3,256,256]{2,1,0:T(8,128)}), (f32[256,256]{1,0:T(8,128)}, f32[3,256,256]{2,1,0:T(8,128)})) %all-reduce.10.cloned.1.call-update) | async-done | bytes 1048592 | tf_op jit(solution)/shard_map/psum | solution.py:57
  523.2 1.4 select_reduce_fusion
  524.6 2.8 fusion.5
  529.2 0.9 fusion.3
  535.7 1.1 fusion.45
  540.7 1.2 fusion.24
  (59 shorter events, 13.5 us)
Async XLA Ops:
  7.2 3.7 copy-start
  7.2 124.3 %all-reduce.8.cloned.1.call-start = ((), (), s32[]{:S(2)}) async-start(), calls=%async_computation.5 | async-start | bytes 3145728
  9.2 1.6 copy-start.6
  10.8 212.8 %reduce-scatter.2.cloned.1.call-start = ((), (), s32[]{:S(2)}) async-start(), calls=%async_computation.1 | async-start | bytes 4325376 | tf_op jit(solution)/shard_map/reduce_scatter | solution.py:77
  16.0 0.7 copy-start.11
  16.0 116.3 %copy-start.9 = (f32[8,3,320]{2,0,1:T(8,128)S(1)}, f32[8,3,320]{2,0,1:T(8,128)}, u32[]{:S(2)}) copy-start(f32[8,3,320]{2,0,1:T(8,128)} %param.14) | copy-start | bytes 92164
  16.0 116.3 %copy-start.10 = (f32[8,3,320]{2,0,1:T(8,128)S(1)}, f32[8,3,320]{2,0,1:T(8,128)}, u32[]{:S(2)}) copy-start(f32[8,3,320]{2,0,1:T(8,128)} %param.15) | copy-start | bytes 92164
  16.0 143.2 %copy-start.4 = (f32[3,30,320]{2,1,0:T(8,128)S(1)}, f32[3,30,320]{2,1,0:T(8,128)}, u32[]{:S(2)}) copy-start(f32[3,30,320]{2,1,0:T(8,128)} %param.9) | copy-start | bytes 345604
  16.0 279.0 %all-reduce.6.cloned.1.call-start = ((), (), s32[]{:S(2)}) async-start(), calls=%async_computation.4 | async-start | bytes 196608 | tf_op jit(solution)/shard_map/psum | solution.py:93
  132.3 91.4 %copy-start.7 = (f32[8,4000]{1,0:T(8,128)S(1)}, f32[8,4000]{1,0:T(8,128)}, u32[]{:S(2)}) copy-start(f32[8,4000]{1,0:T(8,128)} %param.12) | copy-start | bytes 384004
  132.3 91.4 %copy-start.8 = (f32[8,4000]{1,0:T(8,128)S(1)}, f32[8,4000]{1,0:T(8,128)}, u32[]{:S(2)}) copy-start(f32[8,4000]{1,0:T(8,128)} %param.13) | copy-start | bytes 384004
  161.1 190.9 %all-gather.5.cloned.1.call-start = ((), (), s32[]{:S(2)}) async-start(), calls=%async_computation.3 | async-start | bytes 4325376 | tf_op jit(solution)/shard_map/all_gather | solution.py:85
  223.6 181.9 %all-gather.3.cloned.1.call-start = ((), (), s32[]{:S(2)}) async-start(), calls=%async_computation.2 | async-start | bytes 4325376 | tf_op jit(solution)/shard_map/all_gather | solution.py:84
  225.4 297.8 %all-reduce.10.cloned.1.call-start = ((), (), s32[]{:S(2)}) async-start(), calls=%async_computation.6 | async-start | bytes 2097152 | tf_op jit(solution)/shard_map/psum | solution.py:57
  297.8 84.9 %copy-start.5 = (f32[3,30,256]{2,1,0:T(8,128)S(1)}, f32[3,30,256]{2,1,0:T(8,128)}, u32[]{:S(2)}) copy-start(f32[3,30,256]{2,1,0:T(8,128)} %param.11) | copy-start | bytes 276484
  523.2 4.2 copy-start.1
  531.1 1.0 copy-start.2
  538.6 2.2 copy-start.3
Sparse Core Ops, SparseCore 0:
  11.3 120.1 all-reduce.7
  135.4 88.1 reduce-scatter.1
  226.5 68.4 all-reduce.5
  297.4 54.5 all-gather.4
  355.0 50.4 all-gather.2
  408.6 114.5 all-reduce.9
where the time goes:
time: 549 us
  waiting for transfers between devices  407 us (74%)
  blocking collectives  76.7 us (14%)
  matrix products  41.5 us (8%)
  between operations  15.8 us (3%)
    unnamed x7, waiting for transfers between devices  114 us
    psum x1, waiting for transfers between devices, gram_sums(): return lax.psum((emb_gram, mlp_gram), ('tensor', 'section'))  112 us
    reduce_scatter x1, waiting for transfers between devices, local(): lax.psum_scatter(emb_term, ('tensor', 'section'), scatter_dimension=0, ti...  62.4 us
    all_gather x1, waiting for transfers between devices, local(): lax.all_gather(emb_share, ('tensor', 'section'), axis=0, tiled=True)  54.2 us
    psum x1, waiting for transfers between devices, local(): emb_part, mlp_part = lax.psum((emb_found_block, mlp_found_block), 'shard')  42.7 us
    all_gather x1, blocking collectives, local(): lax.all_gather(mlp_direction, ('tensor', 'section'), axis=0, tiled=True)  26.8 us
    all_gather x1, blocking collectives, local(): lax.all_gather(mlp_share, ('tensor', 'section'), axis=0, tiled=True)  26.2 us
    psum x1, blocking collectives, local(): emb_part, mlp_part = lax.psum((emb_found_block, mlp_found_block), 'shard')  23.7 us
  transfers between devices with their start and end apart: 6, of which 6 were waited for; matrix products, arithmetic and copies ran while one was open for 5% of the time, Pallas kernels for 0%

commit v1 on v0

--- a/solution.py
+++ b/solution.py
@@ -2,6 +2,7 @@
 import jax.numpy as jnp
 from jax import lax
 from jax.sharding import PartitionSpec as P
+from jax.lax import all_to_all, axis_size
 
 NS_STEPS = 3
 coef_a = 3.4445
@@ -81,7 +82,10 @@
     mlp_first_new, mlp_second_new, mlp_direction = adam_moments(mlp_first, mlp_second, mlp_share)
     emb_total = emb_zero
     mlp_total = mlp_zero
-    emb_piece = lax.all_gather(emb_direction, ("tensor", "section"), axis=0, tiled=True)
+    plain = tuple((emb_direction for _ in range(axis_size(("tensor", "section")))))
+    later = jnp.stack(plain, axis=0)
+    w_next = all_to_all(later, axis_name=("tensor", "section"), split_axis=0, concat_axis=0)
+    emb_piece = jnp.concatenate(w_next, 0)
     emb_projected = lax.all_gather(emb_share, ("tensor", "section"), axis=0, tiled=True)
     mlp_piece = lax.all_gather(mlp_direction, ("tensor", "section"), axis=0, tiled=True)
     mlp_projected = lax.all_gather(mlp_share, ("tensor", "section"), axis=0, tiled=True)

time: 549 us -> 527 us (0.960)
  waiting for transfers between devices: 407 us -> 334 us
  blocking collectives: 76.7 us -> 118 us
  starting transfers between devices: 0.24 us -> 7.59 us
    psum x1, waiting for transfers between devices: 42.7 us -> 0.01 us  [local(): emb_part, mlp_part = lax.psum((emb_found_block, mlp_found_block), 'shard')]
    all_gather x1, blocking collectives: 26.8 us -> 68.9 us  [local(): lax.all_gather(mlp_direction, ('tensor', 'section'), axis=0, tiled=True)]
    all_gather x1 -> x0, waiting for transfers between devices: 21.4 us -> none  [local(): lax.all_gather(emb_direction, ('tensor', 'section'), axis=0, tiled=True)]
    all_gather x1, waiting for transfers between devices: 54.2 us -> 45.1 us  [local(): lax.all_gather(emb_share, ('tensor', 'section'), axis=0, tiled=True)]
    all_to_all x0 -> x1, starting transfers between devices: none -> 7.38 us  [local(): all_to_all(later, axis_name=('tensor', 'section'), split_axis=0, concat_a...]
    unnamed x7 -> x6, waiting for transfers between devices: 114 us -> 114 us
  transfers between devices with their start and end apart: 6 -> 6, of which waited for: 6 -> 4; matrix products, arithmetic and copies ran while one was open for 5% -> 6% of each run, Pallas kernels for 0% -> 0%
where the time goes in v1:
time: 527 us
  waiting for transfers between devices  334 us (63%)
  blocking collectives  118 us (22%)
  matrix products  41.8 us (8%)
  between operations  15.5 us (3%)
  starting transfers between devices  7.59 us (1%)
  local copies, waits for them, and re-layouts  5.42 us (1%)
    unnamed x6, waiting for transfers between devices  114 us
    psum x1, waiting for transfers between devices, gram_sums(): return lax.psum((emb_gram, mlp_gram), ('tensor', 'section'))  112 us
    all_gather x1, blocking collectives, local(): lax.all_gather(mlp_direction, ('tensor', 'section'), axis=0, tiled=True)  68.9 us
    reduce_scatter x1, waiting for transfers between devices, local(): lax.psum_scatter(emb_term, ('tensor', 'section'), scatter_dimension=0, ti...  62.5 us
    all_gather x1, waiting for transfers between devices, local(): lax.all_gather(emb_share, ('tensor', 'section'), axis=0, tiled=True)  45.1 us
    all_gather x1, blocking collectives, local(): lax.all_gather(mlp_share, ('tensor', 'section'), axis=0, tiled=True)  26.2 us
    psum x1, blocking collectives, local(): emb_part, mlp_part = lax.psum((emb_found_block, mlp_found_block), 'shard')  23.2 us
  transfers between devices with their start and end apart: 6, of which 4 were waited for; matrix products, arithmetic and copies ran while one was open for 6% of the time, Pallas kernels for 0%

profile of v1, /device:TPU:1, one launch (start us, length us, event | category | flops | bytes accessed | tf_op | source)
XLA Modules:
  0.0 526.8 jit_solution(498048346829355618)
XLA Ops:
  7.2 2.0 convolution_bitcast_fusion.1
  9.3 1.5 copy.31
  10.9 5.0 fusion.35
  17.3 114.2 %all-reduce.8.cloned.1.call-done = f32[256,3,320]{2,1,0:T(4,128)} async-done(((f32[256,3,320]{2,1,0:T(4,128)}), f32[256,3,320]{2,1,0:T(4,128)}) %all-reduce.8.cloned.1.call-update) | async-done | bytes 983056
  133.0 26.2 %all_gather.11 = f32[256,3,320]{2,0,1:T(8,128)S(1)} all-gather(f32[8,3,320]{2,0,1:T(8,128)S(1)} %get-tuple-element.31), channel_id=1, replica_groups=mesh['shard'=8,'tensor'=4,'section'=8] {'tensor','section'}, dimensions={0}, use_global_device_ids=true | all-gather | bytes 1013760 | tf_op jit(solution)/shard_map/all_gather | solution.py:91
  159.2 1.9 convolution_bitcast_fusion.3
  161.1 62.5 %reduce-scatter.2.cloned.1.call-done = f32[8,4000]{1,0:T(8,128)} async-done(((f32[256,4000]{1,0:T(8,128)}), f32[8,4000]{1,0:T(8,128)}) %reduce-scatter.2.cloned.1.call-update) | async-done | bytes 128016 | tf_op jit(solution)/shard_map/reduce_scatter | solution.py:78
  223.6 1.7 add_divide_fusion
  225.3 2.4 stack.2
  227.8 7.4 %all-to-all-start = ((f32[32,8,4000]{2,1,0:T(8,128)}), f32[32,8,4000]{2,1,0:T(8,128)}, u32[]{:S(2)}, u32[]{:S(2)}) async-start(f32[32,8,4000]{2,1,0:T(8,128)} %stack.2), calls=%async_computation.1 | async-start | bytes 8388608 | tf_op jit(solution)/shard_map/all_to_all | solution.py:87
  235.3 68.9 %all_gather.9 = f32[256,3,320]{2,0,1:T(8,128)S(1)} all-gather(f32[8,3,320]{2,0,1:T(8,128)S(1)} %get-tuple-element.28), channel_id=1, replica_groups=mesh['shard'=8,'tensor'=4,'section'=8] {'tensor','section'}, dimensions={0}, use_global_device_ids=true | all-gather | bytes 1013760 | tf_op jit(solution)/shard_map/all_gather | solution.py:90
  304.2 2.8 fusion.42
  306.9 45.1 %all-gather.2.cloned.1.call-done = f32[256,4000]{1,0:T(8,128)} async-done(((f32[8,4000]{1,0:T(8,128)}), f32[256,4000]{1,0:T(8,128)}) %all-gather.2.cloned.1.call-update) | async-done | bytes 4096016 | tf_op jit(solution)/shard_map/all_gather | solution.py:89
  352.0 5.9 %convolution_bitcast_fusion.4 = f32[30,256]{1,0:T(8,128)S(1)} fusion(f32[256,4000]{1,0:T(8,128)} %all-gather.2.cloned.1.call-done, f32[30,4000]{1,0:T(8,128)S(1)} %copy-done), kind=kOutput, calls=%fused_computation.23 | convolution fusion | flops 368640000 | bytes 4606720 | tf_op jit(solution)/shard_map/dv,rv->dr/dot_general | solution.py:95
  357.9 23.2 %psum.28 = f32[30,256]{1,0:T(8,128)S(1)} all-reduce(f32[30,256]{1,0:T(8,128)S(1)} %convolution_bitcast_fusion.4), channel_id=1, replica_groups=mesh['shard'=8,'tensor'=4,'section'=8] {'shard'}, use_global_device_ids=true, to_apply=%region_2.0 | all-reduce | flops 7680 | bytes 61440 | tf_op jit(solution)/shard_map/psum | solution.py:97
  381.0 1.1 fusion.36
  382.2 1.4 convolution_bitcast_fusion.2
  383.6 5.5 %convolution_bitcast_fusion = f32[30,4000]{1,0:T(8,128)} fusion(f32[30,256]{1,0:T(8,128)S(1)} %copy-done.5, f32[32,8,4000]{2,1,0:T(8,128)} %all-to-all-done), kind=kOutput, calls=%fused_computation | convolution fusion | flops 368640000 | bytes 4606720 | tf_op jit(solution)/shard_map/dot_general | solution.py:68
  389.2 112.1 %all-reduce.10.cloned.1.call-done = (f32[256,256]{1,0:T(8,128)}, f32[3,256,256]{2,1,0:T(8,128)}) async-done(((f32[256,256]{1,0:T(8,128)}, f32[3,256,256]{2,1,0:T(8,128)}), (f32[256,256]{1,0:T(8,128)}, f32[3,256,256]{2,1,0:T(8,128)})) %all-reduce.10.cloned.1.call-update) | async-done | bytes 1048592 | tf_op jit(solution)/shard_map/psum | solution.py:58
  501.2 1.7 select_reduce_fusion.1
  503.6 1.5 fusion.10
  505.2 1.3 fusion.20
  508.3 1.1 fusion.6
  519.1 1.2 fusion.25
  (57 shorter events, 13.7 us)
Async XLA Ops:
  7.2 3.7 copy-start
  7.2 3.7 copy-start.5
  7.2 124.3 %all-reduce.8.cloned.1.call-start = ((), (), s32[]{:S(2)}) async-start(), calls=%async_computation.5 | async-start | bytes 3145728
  10.8 5.2 copy-start.10
  10.8 121.5 %copy-start.8 = (f32[8,3,320]{2,0,1:T(8,128)S(1)}, f32[8,3,320]{2,0,1:T(8,128)}, u32[]{:S(2)}) copy-start(f32[8,3,320]{2,0,1:T(8,128)} %param.14) | copy-start | bytes 92164
  10.8 121.5 %copy-start.9 = (f32[8,3,320]{2,0,1:T(8,128)S(1)}, f32[8,3,320]{2,0,1:T(8,128)}, u32[]{:S(2)}) copy-start(f32[8,3,320]{2,0,1:T(8,128)} %param.15) | copy-start | bytes 92164
  10.8 148.4 %copy-start.3 = (f32[3,30,320]{2,1,0:T(8,128)S(1)}, f32[3,30,320]{2,1,0:T(8,128)}, u32[]{:S(2)}) copy-start(f32[3,30,320]{2,1,0:T(8,128)} %param.9) | copy-start | bytes 345604
  10.9 212.7 %reduce-scatter.2.cloned.1.call-start = ((), (), s32[]{:S(2)}) async-start(), calls=%async_computation.2 | async-start | bytes 4325376 | tf_op jit(solution)/shard_map/reduce_scatter | solution.py:78
  16.0 207.7 %copy-start.6 = (f32[8,4000]{1,0:T(8,128)S(1)}, f32[8,4000]{1,0:T(8,128)}, u32[]{:S(2)}) copy-start(f32[8,4000]{1,0:T(8,128)} %param.12) | copy-start | bytes 384004
  16.0 207.7 %copy-start.7 = (f32[8,4000]{1,0:T(8,128)S(1)}, f32[8,4000]{1,0:T(8,128)}, u32[]{:S(2)}) copy-start(f32[8,4000]{1,0:T(8,128)} %param.13) | copy-start | bytes 384004
  16.0 288.2 %all-reduce.6.cloned.1.call-start = ((), (), s32[]{:S(2)}) async-start(), calls=%async_computation.4 | async-start | bytes 196608 | tf_op jit(solution)/shard_map/psum | solution.py:97
  161.1 190.9 %all-gather.2.cloned.1.call-start = ((), (), s32[]{:S(2)}) async-start(), calls=%async_computation.3 | async-start | bytes 4325376 | tf_op jit(solution)/shard_map/all_gather | solution.py:89
  227.8 155.9 %all-to-all-start = ((f32[32,8,4000]{2,1,0:T(8,128)}), f32[32,8,4000]{2,1,0:T(8,128)}, u32[]{:S(2)}, u32[]{:S(2)}) async-start(f32[32,8,4000]{2,1,0:T(8,128)} %stack.2), calls=%async_computation.1 | async-start | bytes 8388608 | tf_op jit(solution)/shard_map/all_to_all | solution.py:87
  235.2 266.1 %all-reduce.10.cloned.1.call-start = ((), (), s32[]{:S(2)}) async-start(), calls=%async_computation.6 | async-start | bytes 2097152 | tf_op jit(solution)/shard_map/psum | solution.py:58
  235.3 146.9 %copy-start.4 = (f32[3,30,256]{2,1,0:T(8,128)S(1)}, f32[3,30,256]{2,1,0:T(8,128)}, u32[]{:S(2)}) copy-start(f32[3,30,256]{2,1,0:T(8,128)} %param.11) | copy-start | bytes 276484
  501.2 6.9 %copy-start.1 = (f32[3,256,256]{2,1,0:T(8,128)S(1)}, f32[3,256,256]{2,1,0:T(8,128)}, u32[]{:S(2)}) copy-start(f32[3,256,256]{2,1,0:T(8,128)} %get-tuple-element.25) | copy-start | bytes 2359300
  515.1 4.0 copy-start.2
Sparse Core Ops, SparseCore 0:
  11.3 120.1 all-reduce.7
  135.4 88.1 reduce-scatter.1
  226.5 68.7 all-reduce.5
  297.7 54.2 all-gather.1
  382.3 118.8 all-reduce.9
